TPU v7x, 512 devices: a whole 4x4x16 slice. The times are simulated.
512 devices in a mesh: section: 8 (over x, core), dp: 64 (over y, z).
Axes of the slice: x: 4, y: 4, z: 16, core: 2. Of those that a mesh axis runs over, the one named last changes fastest.
Arguments:
- activations: bfloat16 [8, 8192, 5120], P('section', 'dp'), may hold values from -200 to 200, as said below
- upstream: bfloat16 [8, 8192, 5120], P('section', 'dp'), may hold values from -120 to 120, as said below
- section_norm_gain: float32 [8, 5120], P('section'), may hold values from 0.1 to 1.9
- adapter_down_weight: bfloat16 [8, 16, 5120], P('section'), may hold values from -0.078125 to 0.078125
- adapter_up_weight: bfloat16 [8, 16, 5120], P('section'), may hold values from -0.078125 to 0.078125
Outputs:
- passed: bfloat16 [8, 8192, 5120], P('section', 'dp')
- grad_pair: bfloat16 [8, 163840], P('section', 'dp')
Inputs may be any that keep to these rules, and one draw needn't show every extreme that they name: `activations`: activations of one token position share a part across replicas; rows and features have different scales. `upstream`: gradients of one token position share a part across replicas.
All inputs are finite; a program needn't handle non-finite values.
Results may differ from a plain program's by a relative error of at most 0.0034.
Values may be sent and summed in bfloat16 or wider, within the bound.
No kernel may reach another device: no remote copies, remote signals or barrier semaphores. Data moves between devices by JAX's collectives and lax.ppermute only.
A program may use at most 64 MiB of HBM per device.

v0:
```python
import jax
import jax.numpy as jnp
from jax import lax
from jax.sharding import PartitionSpec as P

norm_eps = 1e-05
pair_eps = 1e-06
adapter_scale = 2.0
HIGH = lax.Precision.HIGHEST


def from_behind(x, axis, by):
    size = lax.axis_size(axis)
    pairs = [(i, i + by) for i in range(size) if 0 <= i + by < size]
    return lax.ppermute(x, axis, pairs)


def replica_backward(inputs, incoming_gradient, gain_row, down_rows, upward_rows):
    widened = inputs.astype(jnp.float32)
    inverse = lax.rsqrt(jnp.mean(widened * widened, axis=-1, keepdims=True) + norm_eps)
    scaled = widened * inverse
    normed = (scaled * gain_row).astype(jnp.bfloat16)
    reduced_gradient = jnp.einsum(
        "sh,gh->sg", normed, down_rows, preferred_element_type=jnp.float32
    ).astype(jnp.bfloat16)
    count_of_rows = inputs.shape[0]
    upward_term = (
        adapter_scale
        * jnp.einsum(
            "tk,td->kd", reduced_gradient, incoming_gradient, preferred_element_type=jnp.float32
        )
        / count_of_rows
    )
    backward_lowrank = (
        adapter_scale
        * jnp.einsum(
            "sh,gh->sg", incoming_gradient, upward_rows, preferred_element_type=jnp.float32
        )
    ).astype(jnp.bfloat16)
    down_term = (
        jnp.einsum("tk,td->kd", backward_lowrank, normed, preferred_element_type=jnp.float32)
        / count_of_rows
    )
    back_norm = (
        jnp.einsum("tk,kd->td", backward_lowrank, down_rows, preferred_element_type=jnp.float32)
        * gain_row
    )
    centre = jnp.mean(back_norm * scaled, axis=-1, keepdims=True)
    passed = incoming_gradient.astype(jnp.float32) + inverse * (back_norm - scaled * centre)
    return (passed.astype(jnp.bfloat16), jnp.stack([down_term, upward_term]))


def swap_rows(c, level_bit):
    t, n = (c.shape[0], c.shape[1])
    rest = c.shape[2:]
    g = c.reshape((t, n // 2 ** (level_bit + 1), 2, 2**level_bit) + rest)
    return g[:, :, ::-1].reshape(c.shape)


def coefficient_tree(gram):
    tensors, n = (gram.shape[0], gram.shape[1])
    coef = jnp.broadcast_to(jnp.eye(n, dtype=jnp.float32), (tensors, n, n))
    for level_bit in range(n.bit_length() - 1):
        partner = swap_rows(coef, level_bit)
        gc = jnp.einsum("tra,tab->trb", coef, gram, precision=HIGH)
        inner_sum = jnp.sum(gc * partner, axis=-1, keepdims=True)
        own_square = jnp.sum(gc * coef, axis=-1, keepdims=True)
        far_square = swap_rows(own_square, level_bit)
        keep_coef = 1.0 - inner_sum / (2.0 * (own_square + pair_eps))
        take_coef = 1.0 - inner_sum / (2.0 * (far_square + pair_eps))
        coef = keep_coef * coef + take_coef * partner
    return coef[:, 0, :]


def gram_adasum(grad_pair):
    devices = lax.axis_size("dp")
    me = lax.axis_index("dp")
    flat = grad_pair.reshape(devices, -1)
    chunks = lax.all_to_all(flat, "dp", 0, 0, tiled=True)
    tensors = grad_pair.shape[0]
    per_tensor = devices // tensors
    mine = me // per_tensor
    partial = jnp.dot(chunks, chunks.T, precision=HIGH, preferred_element_type=jnp.float32)
    slot = (jnp.arange(tensors) == mine)[:, None, None]
    gram = lax.psum(jnp.where(slot, partial[None], 0.0), "dp")
    coef = coefficient_tree(gram)
    own_coef = jnp.sum(jnp.where((jnp.arange(tensors) == mine)[:, None], coef, 0.0), axis=0)
    combined = jnp.sum(own_coef[:, None] * chunks, axis=0)
    return combined.astype(jnp.bfloat16)[None]


def per_device(activations, upstream, section_norm_gain, adapter_down_weight, adapter_up_weight):
    passed_local, grad_pair = replica_backward(
        activations[0],
        upstream[0],
        section_norm_gain[0],
        adapter_down_weight[0],
        adapter_up_weight[0],
    )
    shifted = from_behind(passed_local[None], "section", -1)
    merged_gradient = gram_adasum(grad_pair)
    return (shifted, merged_gradient)


def solution(mesh):
    return jax.shard_map(
        per_device,
        mesh=mesh,
        in_specs=(
            P("section", "dp", None),
            P("section", "dp", None),
            P("section", None),
            P("section", None, None),
            P("section", None, None),
        ),
        out_specs=(P("section", "dp", None), P("section", "dp")),
        check_vma=False,
    )
```

profile of v0, /device:TPU:6, one launch (start us, length us, event | category | flops | bytes accessed | tf_op | source)
XLA Modules:
  0.0 352.2 jit_solution(4884689482944939448)
XLA Ops:
  0.7 1.8 fusion.13
  2.5 1.8 fusion.31
  4.3 1.9 fusion
  6.2 0.5 fusion.1
  6.7 0.5 copy-done.3
  7.2 1.6 all_to_all.11
  8.8 18.7 %all-to-all-start = ((f32[64,1,2560]{2,1,0:T(1,128)}), f32[64,1,2560]{2,1,0:T(1,128)S(1)}, u32[]{:S(2)}, u32[]{:S(2)}) async-start(f32[64,1,2560]{2,1,0:T(1,128)} %all_to_all.11), calls=%async_computation | async-start | bytes 1310720 | tf_op jit(solution)/shard_map/all_to_all | solution.py:79
  27.5 0.7 fusion.7
  28.2 1.9 fusion.20
  30.1 1.9 collective-permute-start
  32.6 0.1 fusion.59
  32.7 0.1 compare_convert_fusion
  32.8 14.6 %collective-permute-done = bf16[1,128,5120]{2,1,0:T(8,128)(2,1)S(1)} collective-permute-done((bf16[1,128,5120]{2,1,0:T(8,128)(2,1)}, bf16[1,128,5120]{2,1,0:T(8,128)(2,1)S(1)}, u32[]{:S(2)}, u32[]{:S(2)}) %collective-permute-start) | collective-permute-done | bytes 1310752 | tf_op jit(solution)/shard_map/ppermute | solution.py:15
  47.5 17.5 %all-to-all-done = f32[64,1,2560]{2,1,0:T(1,128)S(1)} async-done(((f32[64,1,2560]{2,1,0:T(1,128)}), f32[64,1,2560]{2,1,0:T(1,128)S(1)}, u32[]{:S(2)}, u32[]{:S(2)}) %all-to-all-start) | async-done | bytes 655392 | tf_op jit(solution)/shard_map/all_to_all | solution.py:79
  64.9 0.7 fusion.39
  65.7 274.8 %psum.7 = f32[2,64,64]{1,2,0:T(8,128)S(1)} all-reduce(f32[2,64,64]{1,2,0:T(8,128)S(1)} %broadcast_select_fusion), channel_id=1, replica_groups=mesh['section'=8,'dp'=64] {'dp'}, use_global_device_ids=true, to_apply=%region_2.3 | all-reduce | flops 8192 | bytes 65536 | tf_op jit(solution)/shard_map/psum | solution.py:85
  340.5 0.2 multiply_reduce_fusion.10
  340.7 0.1 reduce_sum.178
  340.9 0.1 reduce_sum.182
  341.0 0.1 reshape_broadcast_in_dim.18
  341.2 0.1 mul.669
  341.3 0.1 mul.672
  341.4 0.1 mul.689
  341.6 0.1 copy.128
  341.7 0.1 copy.129
  341.8 0.1 copy.133
  341.9 0.1 copy.134
  342.0 0.1 copy.130
  342.1 0.2 multiply_add_fusion.6
  342.3 0.2 rev.38
  342.7 0.2 multiply_reduce_fusion.8
  342.9 0.1 reshape_broadcast_in_dim.19
  343.1 0.1 reshape.734
  343.2 0.1 mul.684
  343.3 0.1 reduce_sum.181
  343.5 0.1 mul.687
  343.6 0.2 fusion.50
  344.0 0.2 multiply_reduce_fusion.6
  344.2 0.1 reshape_broadcast_in_dim.20
  344.4 0.1 mul.705
  344.5 0.1 mul.723
  344.6 0.1 mul.712
  344.8 0.1 reduce_sum.186
  344.9 0.1 mul.719
  345.1 0.1 reduce_sum.185
  345.3 0.2 multiply_add_fusion.3
  345.6 0.2 multiply_reduce_fusion.4
  345.9 0.1 reshape_broadcast_in_dim.21
  346.0 0.1 mul.732
  346.3 0.1 mul.752
  346.6 0.1 mul.744
  346.8 0.1 mul.748
  347.2 0.2 multiply_add_fusion.1
  347.6 0.2 multiply_reduce_fusion.2
  348.5 0.1 mul.787
  348.7 0.1 mul.779
  348.9 0.1 mul.783
  349.3 0.2 fusion.49
  349.7 0.2 multiply_reduce_fusion
  350.2 0.1 fusion.48
  350.3 0.1 select_reduce_fusion
  350.4 0.1 fusion.41
  350.5 0.6 convert_element_type.85
  351.1 1.1 copy.181
  (103 shorter events, 4.3 us)
Async XLA Ops:
  0.6 3.6 %copy-start = (bf16[1,16,5120]{2,1,0:T(8,128)(2,1)S(1)}, bf16[1,16,5120]{2,1,0:T(8,128)(2,1)}, u32[]{:S(2)}) copy-start(bf16[1,16,5120]{2,1,0:T(8,128)(2,1)} %param.8) | copy-start | bytes 491524
  0.6 3.6 %copy-start.1 = (bf16[1,128,5120]{2,1,0:T(8,128)(2,1)S(1)}, bf16[1,128,5120]{2,1,0:T(8,128)(2,1)}, u32[]{:S(2)}) copy-start(bf16[1,128,5120]{2,1,0:T(8,128)(2,1)} %param.5) | copy-start | bytes 3932164
  0.7 3.6 %copy-start.2 = (bf16[1,128,5120]{2,1,0:T(8,128)(2,1)S(1)}, bf16[1,128,5120]{2,1,0:T(8,128)(2,1)}, u32[]{:S(2)}) copy-start(bf16[1,128,5120]{2,1,0:T(8,128)(2,1)} %param.6) | copy-start | bytes 3932164
  0.7 3.6 %copy-start.4 = (f32[1,5120]{1,0:T(1,128)S(1)}, f32[1,5120]{1,0:T(1,128)}, u32[]{:S(2)}) copy-start(f32[1,5120]{1,0:T(1,128)} %param.7) | copy-start | bytes 61444
  6.2 1.0 copy-start.3
  8.8 56.1 %all-to-all-start = ((f32[64,1,2560]{2,1,0:T(1,128)}), f32[64,1,2560]{2,1,0:T(1,128)S(1)}, u32[]{:S(2)}, u32[]{:S(2)}) async-start(f32[64,1,2560]{2,1,0:T(1,128)} %all_to_all.11), calls=%async_computation | async-start | bytes 1310720 | tf_op jit(solution)/shard_map/all_to_all | solution.py:79
  30.1 17.3 %collective-permute-start = (bf16[1,128,5120]{2,1,0:T(8,128)(2,1)}, bf16[1,128,5120]{2,1,0:T(8,128)(2,1)S(1)}, u32[]{:S(2)}, u32[]{:S(2)}) collective-permute-start(bf16[1,128,5120]{2,1,0:T(8,128)(2,1)} %fusion.20), channel_id=1, source_target_pairs={{64,0},{128,64},{192,128},{256,192},{320,256},{384,320},{448,384},... | collective-permute-start | bytes 3932168 | tf_op jit(solution)/shard_map/ppermute | solution.py:15
where the time goes:
time: 352 us
  blocking collectives  275 us (78%)
  waiting for transfers between devices  32.1 us (9%)
  starting transfers between devices  20.6 us (6%)
  local copies, waits for them, and re-layouts  10.4 us (3%)
  matrix products  6.79 us (2%)
  other arithmetic  6.14 us (2%)
    psum x1, blocking collectives, gram_adasum(): gram = lax.psum(jnp.where(slot, partial[None], 0.0), 'dp')  275 us
    all_to_all x1, starting transfers between devices, gram_adasum(): chunks = lax.all_to_all(flat, 'dp', 0, 0, tiled=True)  18.7 us
    all_to_all x1, waiting for transfers between devices, gram_adasum(): chunks = lax.all_to_all(flat, 'dp', 0, 0, tiled=True)  17.5 us
    ppermute x1, waiting for transfers between devices, from_behind(): return lax.ppermute(x, axis, pairs)  14.6 us
  transfers between devices with their start and end apart: 2, of which 2 were waited for; matrix products, arithmetic and copies ran while one was open for 1% of the time, Pallas kernels for 0%

commit v1 on v0

--- a/solution.py
+++ b/solution.py
@@ -82,7 +82,7 @@
     mine = me // per_tensor
     partial = jnp.dot(chunks, chunks.T, precision=HIGH, preferred_element_type=jnp.float32)
     slot = (jnp.arange(tensors) == mine)[:, None, None]
-    gram = lax.psum(jnp.where(slot, partial[None], 0.0), "dp")
+    gram = jnp.sum(lax.all_gather(jnp.where(slot, partial[None], 0.0), "dp"), axis=0)
     coef = coefficient_tree(gram)
     own_coef = jnp.sum(jnp.where((jnp.arange(tensors) == mine)[:, None], coef, 0.0), axis=0)
     combined = jnp.sum(own_coef[:, None] * chunks, axis=0)

time: 352 us -> 235 us (0.67)
  blocking collectives: 275 us -> 0 us
  waiting for transfers between devices: 32.1 us -> 171 us
  between operations: 1.28 us -> 14.7 us
  other arithmetic: 6.14 us -> 10.4 us
    psum x1 -> x0, blocking collectives: 275 us -> none  [gram_adasum(): gram = lax.psum(jnp.where(slot, partial[None], 0.0), 'dp')]
    all_gather x0 -> x1, waiting for transfers between devices: none -> 119 us  [gram_adasum(): lax.all_gather(jnp.where(slot, partial[None], 0.0), 'dp')]
    all_to_all x1, waiting for transfers between devices: 17.5 us -> 37.3 us  [gram_adasum(): chunks = lax.all_to_all(flat, 'dp', 0, 0, tiled=True)]
  transfers between devices with their start and end apart: 2 -> 3, of which waited for: 2 -> 3; matrix products, arithmetic and copies ran while one was open for 1% -> 1% of each run, Pallas kernels for 0% -> 0%
where the time goes in v1:
time: 235 us; the launch traced here: 234 us
  waiting for transfers between devices  171 us (73%)
  starting transfers between devices  20.7 us (9%)
  between operations  14.7 us (6%)
  other arithmetic  10.4 us (4%)
  local copies, waits for them, and re-layouts  9.89 us (4%)
  matrix products  7.97 us (3%)
    all_gather x1, waiting for transfers between devices, gram_adasum(): lax.all_gather(jnp.where(slot, partial[None], 0.0), 'dp')  119 us
    all_to_all x1, waiting for transfers between devices, gram_adasum(): chunks = lax.all_to_all(flat, 'dp', 0, 0, tiled=True)  37.3 us
    all_to_all x1, starting transfers between devices, gram_adasum(): chunks = lax.all_to_all(flat, 'dp', 0, 0, tiled=True)  18.7 us
    ppermute x1, waiting for transfers between devices, from_behind(): return lax.ppermute(x, axis, pairs)  14.7 us
  transfers between devices with their start and end apart: 3, of which 3 were waited for; matrix products, arithmetic and copies ran while one was open for 1% of the time, Pallas kernels for 0%

profile of v1, /device:TPU:6, one launch (start us, length us, event | category | flops | bytes accessed | tf_op | source)
XLA Modules:
  0.0 234.2 jit_solution(15056871511195180932)
XLA Ops:
  7.2 1.8 fusion.13
  9.0 1.8 fusion.31
  10.8 1.2 fusion.1
  12.0 1.9 fusion
  13.9 1.1 pad_maximum_fusion
  15.0 1.6 all_to_all.11
  16.6 18.7 %all-to-all-start = ((f32[64,1,2560]{2,1,0:T(1,128)}), f32[64,1,2560]{2,1,0:T(1,128)S(1)}, u32[]{:S(2)}, u32[]{:S(2)}) async-start(f32[64,1,2560]{2,1,0:T(1,128)} %all_to_all.11), calls=%async_computation | async-start | bytes 1310720 | tf_op jit(solution)/shard_map/all_to_all | solution.py:79
  35.4 37.3 %all-to-all-done = f32[64,1,2560]{2,1,0:T(1,128)S(1)} async-done(((f32[64,1,2560]{2,1,0:T(1,128)}), f32[64,1,2560]{2,1,0:T(1,128)S(1)}, u32[]{:S(2)}, u32[]{:S(2)}) %all-to-all-start) | async-done | bytes 655392 | tf_op jit(solution)/shard_map/all_to_all | solution.py:79
  72.8 0.7 fusion.39
  73.4 0.7 broadcast_select_fusion
  74.2 0.7 fusion.7
  74.8 1.9 fusion.20
  76.7 1.9 collective-permute-start
  79.2 0.1 fusion.59
  79.3 0.1 compare_convert_fusion
  79.4 14.7 %collective-permute-done = bf16[1,128,5120]{2,1,0:T(8,128)(2,1)S(1)} collective-permute-done((bf16[1,128,5120]{2,1,0:T(8,128)(2,1)}, bf16[1,128,5120]{2,1,0:T(8,128)(2,1)S(1)}, u32[]{:S(2)}, u32[]{:S(2)}) %collective-permute-start) | collective-permute-done | bytes 1310752 | tf_op jit(solution)/shard_map/ppermute | solution.py:15
  94.1 118.6 %all-gather.2.cloned.1.call-done = f32[64,2,64,64]{3,2,1,0:T(8,128)} async-done(((f32[1,2,64,64]{3,2,1,0:T(8,128)}), f32[64,2,64,64]{3,2,1,0:T(8,128)}) %all-gather.2.cloned.1.call-update) | async-done | bytes 2097168 | tf_op jit(solution)/shard_map/all_gather | solution.py:85
  212.7 2.6 %reduce_sum.185 = f32[2,64,64]{2,1,0:T(8,128)S(1)} reduce(f32[64,2,64,64]{3,2,1,0:T(8,128)} %all-gather.2.cloned.1.call-done, f32[]{:T(128)} %constant.38.clone.1), dimensions={0}, to_apply=%region_2.3 | reduce | flops 516096 | bytes 2129924 | tf_op jit(solution)/shard_map/reduce_sum | solution.py:85
  215.2 0.3 multiply_reduce_fusion.10
  215.5 0.1 reshape_broadcast_in_dim.18
  215.7 0.1 mul.669
  215.8 0.1 reduce_sum.188
  216.0 0.1 mul.672
  216.1 0.1 copy.168
  216.2 0.1 copy.172
  216.3 0.1 copy.167
  216.5 0.1 copy.169
  216.6 0.1 copy.173
  216.7 0.2 multiply_add_fusion.6
  216.9 0.2 rev.38
  217.2 0.3 multiply_reduce_fusion.8
  217.5 0.1 reshape_broadcast_in_dim.19
  217.7 0.1 mul.684
  217.8 0.1 mul.748
  218.0 0.1 mul.744
  218.4 0.1 mul.687
  218.5 0.1 reshape.737
  218.6 0.1 reduce_sum.191
  218.7 0.1 mul.689
  218.9 0.1 reduce_sum.192
  219.0 0.2 fusion.50
  219.4 0.3 multiply_reduce_fusion.6
  219.7 0.1 reshape_broadcast_in_dim.20
  219.8 0.1 mul.705
  219.9 0.1 mul.752
  220.1 0.1 mul.719
  220.3 0.1 mul.712
  220.5 0.1 reduce_sum.197
  220.9 0.1 mul.723
  221.1 0.2 multiply_add_fusion.3
  221.4 0.3 multiply_reduce_fusion.4
  221.8 0.1 mul.732
  222.1 0.1 mul.783
  222.4 0.1 mul.779
  222.6 0.1 mul.787
  223.3 0.2 multiply_add_fusion.1
  223.6 0.3 multiply_reduce_fusion.2
  224.5 0.2 fusion.49
  224.8 0.3 multiply_reduce_fusion
  225.4 0.1 fusion.48
  225.5 0.1 select_reduce_fusion
  225.6 0.1 fusion.41
  225.7 0.6 convert_element_type.85
  226.3 1.1 copy.229
  (104 shorter events, 4.4 us)
Async XLA Ops:
  7.2 4.9 %copy-start = (bf16[1,16,5120]{2,1,0:T(8,128)(2,1)S(1)}, bf16[1,16,5120]{2,1,0:T(8,128)(2,1)}, u32[]{:S(2)}) copy-start(bf16[1,16,5120]{2,1,0:T(8,128)(2,1)} %param.8) | copy-start | bytes 491524
  7.2 3.6 %copy-start.1 = (bf16[1,128,5120]{2,1,0:T(8,128)(2,1)S(1)}, bf16[1,128,5120]{2,1,0:T(8,128)(2,1)}, u32[]{:S(2)}) copy-start(bf16[1,128,5120]{2,1,0:T(8,128)(2,1)} %param.5) | copy-start | bytes 3932164
  7.2 4.8 %copy-start.2 = (bf16[1,128,5120]{2,1,0:T(8,128)(2,1)S(1)}, bf16[1,128,5120]{2,1,0:T(8,128)(2,1)}, u32[]{:S(2)}) copy-start(bf16[1,128,5120]{2,1,0:T(8,128)(2,1)} %param.6) | copy-start | bytes 3932164
  7.2 3.6 %copy-start.3 = (f32[1,5120]{1,0:T(1,128)S(1)}, f32[1,5120]{1,0:T(1,128)}, u32[]{:S(2)}) copy-start(f32[1,5120]{1,0:T(1,128)} %param.7) | copy-start | bytes 61444
  16.6 56.1 %all-to-all-start = ((f32[64,1,2560]{2,1,0:T(1,128)}), f32[64,1,2560]{2,1,0:T(1,128)S(1)}, u32[]{:S(2)}, u32[]{:S(2)}) async-start(f32[64,1,2560]{2,1,0:T(1,128)} %all_to_all.11), calls=%async_computation | async-start | bytes 1310720 | tf_op jit(solution)/shard_map/all_to_all | solution.py:79
  35.4 177.3 %all-gather.2.cloned.1.call-start = ((), (), s32[]{:S(2)}) async-start(), calls=%async_computation.1 | async-start | bytes 4259840 | tf_op jit(solution)/shard_map/all_gather | solution.py:85
  76.7 17.3 %collective-permute-start = (bf16[1,128,5120]{2,1,0:T(8,128)(2,1)}, bf16[1,128,5120]{2,1,0:T(8,128)(2,1)S(1)}, u32[]{:S(2)}, u32[]{:S(2)}) collective-permute-start(bf16[1,128,5120]{2,1,0:T(8,128)(2,1)} %fusion.20), channel_id=1, source_target_pairs={{64,0},{128,64},{192,128},{256,192},{320,256},{384,320},{448,384},... | collective-permute-start | bytes 3932168 | tf_op jit(solution)/shard_map/ppermute | solution.py:15
Sparse Core Ops, SparseCore 0:
  74.3 138.3 all-gather.1
